TPU v7x, 128 devices: a whole 4x4x4 slice. The times are simulated.
128 devices in a mesh: pr: 8 (over z, core), pc: 16 (over y, x).
Axes of the slice: x: 4, y: 4, z: 4, core: 2. Of those that a mesh axis runs over, the one named last changes fastest.
Arguments:
- test_points: bfloat16 [131072, 512], P('pr'), may hold values from -15 to 15
- panel_points: bfloat16 [1024, 512], P('pc'), may hold values from -15 to 15
- factor_rows: float32 [1024, 32768], P('pc', 'pr'), may hold values from -0.03125 to 0.03125
- alpha_below: float32 [32768, 128], P(('pr', 'pc')), may hold values from -6 to 6
- targets: float32 [1024, 128], P('pc'), may hold values from -6 to 6
- inverse_block: float32 [1024, 1024], P('pc'), may hold values from -0.008 to 0.08, as said below
- predictions_in: float32 [131072, 128], P(('pr', 'pc')), may hold values from -6 to 6
Outputs:
- predictions: float32 [131072, 128], P(('pr', 'pc'))
Inputs may be any that keep to these rules, and one draw needn't show every extreme that they name: `inverse_block`: lower triangular with a positive diagonal.
All inputs are finite; a program needn't handle non-finite values.
Results may differ from a plain program's by a relative error of at most 0.0003.
Values may be sent and summed in bfloat16 or wider, within the bound.
No kernel may reach another device: no remote copies, remote signals or barrier semaphores. Data moves between devices by JAX's collectives and lax.ppermute only.
A program may use at most 128 MiB of HBM per device.

v0:
```python
import math
import jax
import jax.numpy as jnp
from jax import lax
from jax.sharding import PartitionSpec as P

LAYERS = 4
bias_var = 0.1
weight_var = 2.0


def arc_kernel(panel, test, test_norms):
    width = panel.shape[1]
    cross = jnp.dot(panel, test.T, preferred_element_type=jnp.float32) / width
    panel_var = jnp.einsum("pd,pd->p", panel, panel, preferred_element_type=jnp.float32) / width
    kern = bias_var + weight_var * cross
    panel_k = bias_var + weight_var * panel_var
    test_k = bias_var + weight_var * (test_norms / width)
    for level in range(LAYERS):
        spread = jnp.sqrt(panel_k[:, None] * test_k[None, :])
        cosine = kern / spread
        theta = jnp.arccos(cosine)
        kern = bias_var + weight_var / (2.0 * math.pi) * spread * (
            jnp.sqrt(1.0 - cosine * cosine) + (math.pi - theta) * cosine
        )
        panel_k = bias_var + 0.5 * weight_var * panel_k
        test_k = bias_var + 0.5 * weight_var * test_k
    return kern


def contract_rows(left, right):
    return lax.dot_general(
        left,
        right,
        (((0,), (0,)), ((), ())),
        precision=lax.Precision.HIGHEST,
        preferred_element_type=jnp.float32,
    )


def body(
    test_points, panel_points, factor_rows, alpha_below, targets, inverse_block, predictions_in
):
    rows = predictions_in.shape[0]
    own = lax.axis_index("pc")
    partial_sum = jnp.dot(
        factor_rows,
        lax.all_gather(alpha_below, "pc", axis=0, tiled=True),
        precision=lax.Precision.HIGHEST,
        preferred_element_type=jnp.float32,
    )
    carried = lax.psum(partial_sum, "pr")
    residual = targets - carried
    alpha_panel = lax.psum(contract_rows(inverse_block, residual), "pc")
    panel_all = lax.all_gather(panel_points, "pc", axis=0, tiled=True)
    test_own = lax.dynamic_slice_in_dim(test_points, own * rows, rows, 0)
    test_norms = jnp.einsum("nd,nd->n", test_own, test_own, preferred_element_type=jnp.float32)
    kern = lax.optimization_barrier(arc_kernel(panel_all, test_own, test_norms))
    update = contract_rows(kern, alpha_panel)
    return predictions_in + update


def solution(mesh):
    placed = (
        P("pr", None),
        P("pc", None),
        P("pc", "pr"),
        P(("pr", "pc"), None),
        P("pc", None),
        P("pc", None),
        P(("pr", "pc"), None),
    )
    return jax.shard_map(
        body, mesh=mesh, in_specs=placed, out_specs=P(("pr", "pc"), None), check_vma=False
    )
```

profile of v0, /device:TPU:0, one launch (start us, length us, event | category | flops | bytes accessed | tf_op | source)
XLA Modules:
  0.0 224.8 jit_solution(2418785735525503081)
XLA Ops:
  6.5 0.0 copy-start
  6.5 0.0 copy-start.3
  6.5 0.0 copy-start.4
  6.5 0.0 all-gather.3.cloned.1.call-start
  6.5 0.7 all-gather.3.cloned.1.call-update
  7.3 0.0 all-gather.5.cloned.1.call-start
  7.3 0.7 all-gather.5.cloned.1.call-update
  8.0 0.0 all-reduce.2.cloned.1.call-start
  8.1 1.5 fusion
  9.6 44.7 %all-gather.3.cloned.1.call-done = bf16[1024,512]{1,0:T(8,128)(2,1)} async-done(((bf16[64,512]{1,0:T(8,128)(2,1)}), bf16[1024,512]{1,0:T(8,128)(2,1)}) %all-gather.3.cloned.1.call-update) | async-done | bytes 1048592 | tf_op jit(solution)/shard_map/all_gather | solution.py:55
  54.3 0.0 copy-start.1
  54.3 1.6 fusion.1
  55.9 44.7 %all-gather.5.cloned.1.call-done = f32[4096,128]{1,0:T(8,128)} async-done(((f32[256,128]{1,0:T(8,128)}), f32[4096,128]{1,0:T(8,128)}) %all-gather.5.cloned.1.call-update) | async-done | bytes 2097168 | tf_op jit(solution)/shard_map/all_gather | solution.py:48
  100.6 0.0 copy-done
  100.6 3.0 %fusion.5 = f32[64,128]{1,0:T(8,128)S(1)} fusion(f32[64,4096]{1,0:T(8,128)S(1)} %copy-done, f32[4096,128]{1,0:T(8,128)} %all-gather.5.cloned.1.call-done), kind=kOutput, calls=%fused_computation.19 | convolution fusion | flops 402653184 | bytes 3178496 | tf_op jit(solution)/shard_map/dot_general | solution.py:46
  103.6 24.3 %psum.14 = f32[64,128]{1,0:T(8,128)S(1)} all-reduce(f32[64,128]{1,0:T(8,128)S(1)} %fusion.5), channel_id=1, replica_groups=mesh['pr'=8,'pc'=16] {'pr'}, use_global_device_ids=true, to_apply=%region_0.0 | all-reduce | flops 8192 | bytes 65536 | tf_op jit(solution)/shard_map/psum | solution.py:52
  127.9 0.0 copy-done.3
  127.9 0.0 copy-done.4
  127.9 1.4 convolution_bitcast_fusion
  129.3 0.0 all-reduce.2.cloned.1.call-update
  129.3 0.0 copy-done.1
  129.4 0.0 copy-start.2
  129.4 50.0 %multiply_add_fusion = f32[1024,1024]{0,1:T(8,128)} fusion(bf16[1024,512]{1,0:T(8,128)(2,1)S(1)} %copy-done.1, f32[1024]{0:T(1024)S(1)} %get-tuple-element.12, f32[1024]{0:T(1024)S(1)} %get-tuple-element.8, f32[1024]{0:T(1024)S(1)} %get-tuple-element.11, f32[1024]{0:T(1024)S(1)} %get-tuple-element.7, f32[1024]{0:T(1024)S(1)} %get-tuple-element.10, ...), kind=kOutput, calls=%fused_computation.1 | convolution fusion | flops 1130364928 | bytes 6324228 | tf_op jit(solution)/shard_map/dot_general | solution.py:14
  179.3 32.4 %all-reduce.2.cloned.1.call-done = f32[1024,128]{0,1:T(8,128)} async-done(((f32[1024,128]{0,1:T(8,128)}), f32[1024,128]{0,1:T(8,128)}) %all-reduce.2.cloned.1.call-update) | async-done | bytes 524304 | tf_op jit(solution)/shard_map/psum | solution.py:54
  211.7 0.0 copy-done.2
  211.7 6.5 %convolution_add_fusion = f32[1024,128]{1,0:T(8,128)} fusion(f32[1024,128]{1,0:T(8,128)S(1)} %copy-done.2, f32[1024,1024]{0,1:T(8,128)} %multiply_add_fusion, f32[1024,128]{0,1:T(8,128)} %all-reduce.2.cloned.1.call-done), kind=kOutput, calls=%fused_computation.6 | convolution fusion | flops 1610743808 | bytes 5767168 | tf_op jit(solution)/shard_map/dot_general | solution.py:32
  (2 shorter events, 0.0 us)
Async XLA Ops:
  6.5 94.1 %copy-start = (f32[64,4096]{1,0:T(8,128)S(1)}, f32[64,4096]{1,0:T(8,128)}, u32[]{:S(2)}) copy-start(f32[64,4096]{1,0:T(8,128)} %param.9) | copy-start | bytes 3145732
  6.5 121.4 %copy-start.3 = (f32[64,1024]{1,0:T(8,128)S(1)}, f32[64,1024]{1,0:T(8,128)}, u32[]{:S(2)}) copy-start(f32[64,1024]{1,0:T(8,128)} %param.12) | copy-start | bytes 786436
  6.5 121.4 %copy-start.4 = (f32[64,128]{1,0:T(8,128)S(1)}, f32[64,128]{1,0:T(8,128)}, u32[]{:S(2)}) copy-start(f32[64,128]{1,0:T(8,128)} %param.11) | copy-start | bytes 98308
  6.5 47.8 %all-gather.3.cloned.1.call-start = ((), (), s32[]{:S(2)}) async-start(), calls=%async_computation | async-start | bytes 1114112 | tf_op jit(solution)/shard_map/all_gather | solution.py:55
  7.3 93.4 %all-gather.5.cloned.1.call-start = ((), (), s32[]{:S(2)}) async-start(), calls=%async_computation.1 | async-start | bytes 2228224 | tf_op jit(solution)/shard_map/all_gather | solution.py:48
  8.0 203.7 %all-reduce.2.cloned.1.call-start = ((), (), s32[]{:S(2)}) async-start(), calls=%async_computation.2 | async-start | bytes 1048576 | tf_op jit(solution)/shard_map/psum | solution.py:54
  54.3 75.0 %copy-start.1 = (bf16[1024,512]{1,0:T(8,128)(2,1)S(1)}, bf16[1024,512]{1,0:T(8,128)(2,1)}, u32[]{:S(2)}) copy-start(bf16[1024,512]{1,0:T(8,128)(2,1)} %all-gather.3.cloned.1.call-done) | copy-start | bytes 3145732
  129.4 82.4 %copy-start.2 = (f32[1024,128]{1,0:T(8,128)S(1)}, f32[1024,128]{1,0:T(8,128)}, u32[]{:S(2)}) copy-start(f32[1024,128]{1,0:T(8,128)} %param.13) | copy-start | bytes 1572868
Sparse Core Ops, SparseCore 0:
  9.5 44.8 all-gather.2
  56.5 44.1 all-gather.4
  129.5 82.2 all-reduce.1
where the time goes:
time: 225 us
  waiting for transfers between devices  123 us (55%)
  matrix products  60.9 us (27%)
  blocking collectives  24.3 us (11%)
  between operations  13.2 us (6%)
  other arithmetic  3.1 us (1%)
    dot_general x1, matrix products, arc_kernel(): cross = jnp.dot(panel, test.T, preferred_element_type=jnp.float32) / width  50 us
    all_gather x1, waiting for transfers between devices, body(): panel_all = lax.all_gather(panel_points, 'pc', axis=0, tiled=True)  44.7 us
    all_gather x1, waiting for transfers between devices, body(): lax.all_gather(alpha_below, 'pc', axis=0, tiled=True)  44.7 us
    psum x1, waiting for transfers between devices, body(): alpha_panel = lax.psum(contract_rows(inverse_block, residual), 'pc')  32.4 us
    psum x1, blocking collectives, body(): carried = lax.psum(partial_sum, 'pr')  24.3 us
    dot_general x2, matrix products, contract_rows(): lax.dot_general(left, right, (((0,), (0,)), ((), ())), precision=lax.Prec...  7.94 us
  transfers between devices with their start and end apart: 3, of which 3 were waited for; matrix products, arithmetic and copies ran while one was open for 24% of the time, Pallas kernels for 0%

commit v1 on v0

--- a/solution.py
+++ b/solution.py
@@ -45,7 +45,9 @@
     own = lax.axis_index("pc")
     partial_sum = jnp.dot(
         factor_rows,
-        lax.all_gather(alpha_below, "pc", axis=0, tiled=True),
+        jnp.concatenate(
+            lax.all_to_all(jnp.stack([alpha_below] * lax.axis_size("pc"), 0), "pc", 0, 0), 0
+        ),
         precision=lax.Precision.HIGHEST,
         preferred_element_type=jnp.float32,
     )

time: 225 us -> 191 us (0.85)
  waiting for transfers between devices: 123 us -> 81.1 us
  starting transfers between devices: 0.08 us -> 7.32 us
  local copies, waits for them, and re-layouts: 0.02 us -> 2.46 us
    all_gather x1 -> x0, waiting for transfers between devices: 44.7 us -> none  [body(): lax.all_gather(alpha_below, 'pc', axis=0, tiled=True)]
    all_to_all x0 -> x1, starting transfers between devices: none -> 7.28 us  [body(): lax.all_to_all(jnp.stack([alpha_below] * lax.axis_size('pc'), 0), 'pc', 0...]
    all_gather x1, waiting for transfers between devices: 44.7 us -> 48.6 us  [body(): panel_all = lax.all_gather(panel_points, 'pc', axis=0, tiled=True)]
    another operation x0 -> x1, local copies, waits for them, and re-layouts: none -> 2.44 us  [body(): jnp.stack([alpha_below] * lax.axis_size('pc'), 0)]
  transfers between devices with their start and end apart: 3 -> 3, of which waited for: 3 -> 2; matrix products, arithmetic and copies ran while one was open for 24% -> 29% of each run, Pallas kernels for 0% -> 0%
where the time goes in v1:
time: 191 us
  waiting for transfers between devices  81.1 us (42%)
  matrix products  59.7 us (31%)
  blocking collectives  24 us (13%)
  between operations  13.5 us (7%)
  starting transfers between devices  7.32 us (4%)
  other arithmetic  3.01 us (2%)
  local copies, waits for them, and re-layouts  2.46 us (1%)
    dot_general x1, matrix products, arc_kernel(): cross = jnp.dot(panel, test.T, preferred_element_type=jnp.float32) / width  50.3 us
    all_gather x1, waiting for transfers between devices, body(): panel_all = lax.all_gather(panel_points, 'pc', axis=0, tiled=True)  48.6 us
    psum x1, waiting for transfers between devices, body(): alpha_panel = lax.psum(contract_rows(inverse_block, residual), 'pc')  31.7 us
    psum x1, blocking collectives, body(): carried = lax.psum(partial_sum, 'pr')  24 us
    dot_general x2, matrix products, contract_rows(): lax.dot_general(left, right, (((0,), (0,)), ((), ())), precision=lax.Prec...  7.94 us
    all_to_all x1, starting transfers between devices, body(): lax.all_to_all(jnp.stack([alpha_below] * lax.axis_size('pc'), 0), 'pc', 0...  7.28 us
  transfers between devices with their start and end apart: 3, of which 2 were waited for; matrix products, arithmetic and copies ran while one was open for 29% of the time, Pallas kernels for 0%

profile of v1, /device:TPU:0, one launch (start us, length us, event | category | flops | bytes accessed | tf_op | source)
XLA Modules:
  0.0 191.1 jit_solution(10434228050600634698)
XLA Ops:
  6.5 0.0 copy-start
  6.5 0.0 all-gather.2.cloned.1.call-start
  6.5 0.7 all-gather.2.cloned.1.call-update
  7.3 2.4 %stack.2 = f32[16,256,128]{2,1,0:T(8,128)} broadcast(f32[256,128]{1,0:T(8,128)} %param.10), dimensions={1,2} | broadcast | bytes 2228224 | tf_op jit(solution)/shard_map/stack | solution.py:49
  9.7 0.0 copy-start.2
  9.7 0.0 copy-start.3
  9.7 7.3 %all-to-all-start = ((f32[16,256,128]{2,1,0:T(8,128)}), f32[16,256,128]{2,1,0:T(8,128)S(1)}, u32[]{:S(2)}, u32[]{:S(2)}) async-start(f32[16,256,128]{2,1,0:T(8,128)} %stack.2), calls=%async_computation | async-start | bytes 4194304 | tf_op jit(solution)/shard_map/all_to_all | solution.py:49
  17.0 0.0 all-reduce.2.cloned.1.call-start
  17.0 1.5 fusion
  18.6 48.6 %all-gather.2.cloned.1.call-done = bf16[1024,512]{1,0:T(8,128)(2,1)} async-done(((bf16[64,512]{1,0:T(8,128)(2,1)}), bf16[1024,512]{1,0:T(8,128)(2,1)}) %all-gather.2.cloned.1.call-update) | async-done | bytes 1048592 | tf_op jit(solution)/shard_map/all_gather | solution.py:57
  67.2 1.5 fusion.1
  68.7 0.0 all-to-all-done
  68.7 0.0 copy-done
  68.7 1.4 fusion.5
  70.1 24.0 %psum.14 = f32[64,128]{1,0:T(8,128)S(1)} all-reduce(f32[64,128]{1,0:T(8,128)S(1)} %fusion.5), channel_id=1, replica_groups=mesh['pr'=8,'pc'=16] {'pr'}, use_global_device_ids=true, to_apply=%region_0.0 | all-reduce | flops 8192 | bytes 65536 | tf_op jit(solution)/shard_map/psum | solution.py:54
  94.1 0.0 copy-done.2
  94.2 0.0 copy-done.3
  94.2 1.4 convolution_bitcast_fusion
  95.6 0.0 all-reduce.2.cloned.1.call-update
  95.6 0.0 copy-start.1
  95.6 50.3 %multiply_add_fusion = f32[1024,1024]{0,1:T(8,128)} fusion(bf16[1024,512]{1,0:T(8,128)(2,1)} %all-gather.2.cloned.1.call-done, f32[1024]{0:T(1024)S(1)} %get-tuple-element.12, f32[1024]{0:T(1024)S(1)} %get-tuple-element.8, f32[1024]{0:T(1024)S(1)} %get-tuple-element.11, f32[1024]{0:T(1024)S(1)} %get-tuple-element.7, f32[1024]{0:T(1024)S(1)} %get-tuple-element.10, ...), kind=kOutput, calls=%fused_computation.1 | convolution fusion | flops 1130364928 | bytes 6324228 | tf_op jit(solution)/shard_map/dot_general | solution.py:14
  145.9 31.7 %all-reduce.2.cloned.1.call-done = f32[1024,128]{0,1:T(8,128)} async-done(((f32[1024,128]{0,1:T(8,128)}), f32[1024,128]{0,1:T(8,128)}) %all-reduce.2.cloned.1.call-update) | async-done | bytes 524304 | tf_op jit(solution)/shard_map/psum | solution.py:56
  177.7 0.0 copy-done.1
  177.7 6.5 %convolution_add_fusion = f32[1024,128]{1,0:T(8,128)} fusion(f32[1024,128]{1,0:T(8,128)S(1)} %copy-done.1, f32[1024,1024]{0,1:T(8,128)} %multiply_add_fusion, f32[1024,128]{0,1:T(8,128)} %all-reduce.2.cloned.1.call-done), kind=kOutput, calls=%fused_computation.6 | convolution fusion | flops 1610743808 | bytes 5767168 | tf_op jit(solution)/shard_map/dot_general | solution.py:32
  (2 shorter events, 0.0 us)
Async XLA Ops:
  6.5 62.2 %copy-start = (f32[64,4096]{1,0:T(8,128)S(1)}, f32[64,4096]{1,0:T(8,128)}, u32[]{:S(2)}) copy-start(f32[64,4096]{1,0:T(8,128)} %param.9) | copy-start | bytes 3145732
  6.5 60.6 %all-gather.2.cloned.1.call-start = ((), (), s32[]{:S(2)}) async-start(), calls=%async_computation.1 | async-start | bytes 1114112 | tf_op jit(solution)/shard_map/all_gather | solution.py:57
  9.7 84.4 %copy-start.2 = (f32[64,1024]{1,0:T(8,128)S(1)}, f32[64,1024]{1,0:T(8,128)}, u32[]{:S(2)}) copy-start(f32[64,1024]{1,0:T(8,128)} %param.12) | copy-start | bytes 786436
  9.7 84.4 %copy-start.3 = (f32[64,128]{1,0:T(8,128)S(1)}, f32[64,128]{1,0:T(8,128)}, u32[]{:S(2)}) copy-start(f32[64,128]{1,0:T(8,128)} %param.11) | copy-start | bytes 98308
  9.7 59.0 %all-to-all-start = ((f32[16,256,128]{2,1,0:T(8,128)}), f32[16,256,128]{2,1,0:T(8,128)S(1)}, u32[]{:S(2)}, u32[]{:S(2)}) async-start(f32[16,256,128]{2,1,0:T(8,128)} %stack.2), calls=%async_computation | async-start | bytes 4194304 | tf_op jit(solution)/shard_map/all_to_all | solution.py:49
  17.0 160.7 %all-reduce.2.cloned.1.call-start = ((), (), s32[]{:S(2)}) async-start(), calls=%async_computation.2 | async-start | bytes 1048576 | tf_op jit(solution)/shard_map/psum | solution.py:56
  95.6 82.1 %copy-start.1 = (f32[1024,128]{1,0:T(8,128)S(1)}, f32[1024,128]{1,0:T(8,128)}, u32[]{:S(2)}) copy-start(f32[1024,128]{1,0:T(8,128)} %param.13) | copy-start | bytes 1572868
Sparse Core Ops, SparseCore 0:
  9.5 57.6 all-gather.1
  95.7 81.9 all-reduce.1
